TPU v7x, 128 devices: a whole 4x4x4 slice. The times are simulated.
128 devices in a mesh: seq: 16 (over z, x_lo, core), chan: 4 (over y), rep: 2 (over x_hi).
Axes of the slice: x: 4 (x_hi: 2, x_lo: 2; x = x_hi * 2 + x_lo), y: 4, z: 4, core: 2. Of those that a mesh axis runs over, the one named last changes fastest.
Arguments:
- inputs: bfloat16 [2, 4096, 2048], P('rep', 'seq', 'chan'), may hold values from -6 to 6
- w_in: bfloat16 [2048, 1536], P('chan'), may hold values from -0.25 to 0.25
- w_out: bfloat16 [2048, 2048], P('chan'), may hold values from -0.125 to 0.125
- filt_fwd: float32 [4096, 2048], P('seq', 'chan'), may hold values from -0.09375 to 0.09375
- filt_bwd: float32 [4096, 2048], P('seq', 'chan'), may hold values from -0.09375 to 0.09375
- skip_gain: float32 [2048], P('chan'), may hold values from -4 to 4
- cotangent: bfloat16 [2, 4096, 2048], P('rep', 'seq', 'chan'), may hold values from -6 to 6
Outputs:
- layer_out: bfloat16 [2, 4096, 2048], P('rep', 'seq', 'chan')
- d_input: bfloat16 [2, 4096, 2048], P('rep', 'seq', 'chan')
- d_w_in: float32 [2048, 1536], P('chan')
- d_w_out: float32 [2048, 2048], P('chan')
- d_filt_fwd: float32 [4096, 2048], P('seq', 'chan')
- d_filt_bwd: float32 [4096, 2048], P('seq', 'chan')
- d_skip: float32 [2048], P('chan')
All inputs are finite; a program needn't handle non-finite values.
Results may differ from a plain program's by a relative error of at most 0.005.
Values may be sent and summed in bfloat16 or wider, within the bound.
No kernel may reach another device: no remote copies, remote signals or barrier semaphores. Data moves between devices by JAX's collectives and lax.ppermute only.
A program may use at most 128 MiB of HBM per device.

v0:
```python
import math

import jax
import jax.numpy as jnp
from jax import lax
from jax.sharding import PartitionSpec as P

BLOCK = 512


HIGHEST_PRECISION = lax.Precision.HIGHEST


def wrapped_angle(phase, modulus, factor):
    centered = jnp.where(phase * 2 > modulus, phase - modulus, phase)
    return factor * math.pi / modulus * centered.astype(jnp.float32)


def unit_tables(table_size):
    index_row = jnp.arange(table_size, dtype=jnp.int32)
    phase = index_row[:, None] * index_row[None, :] % table_size
    angle = wrapped_angle(phase, table_size, 2.0)
    return (jnp.cos(angle), jnp.sin(angle))


def table_apply(table, fields, form):
    return jnp.einsum(form, table, fields, precision=HIGHEST_PRECISION)


def rotate(real_part, imag_part, angle):
    cosine = jnp.cos(angle)
    sine = jnp.sin(angle)
    return (real_part * cosine - imag_part * sine, real_part * sine + imag_part * cosine)


def complex_product(left_re, left_im, right_re, right_im):
    return (left_re * right_re - left_im * right_im, left_re * right_im + left_im * right_re)


def regroup(stacked):
    return lax.all_to_all(stacked, "seq", split_axis=1, concat_axis=1, tiled=True)


def forward_transform(fields):
    part_count = lax.axis_size("seq")
    position = lax.axis_index("seq")
    field_count, row_count, chan_width = fields.shape
    block_rows = row_count // part_count
    seq_length = row_count * part_count
    columns = regroup(fields).reshape(field_count, part_count, block_rows, chan_width)
    cos_part, sin_part = unit_tables(part_count)
    real_part = table_apply(cos_part, columns, "kp,fpbc->fkbc")
    imag_part = -table_apply(sin_part, columns, "kp,fpbc->fkbc")
    offsets = position * block_rows + jnp.arange(block_rows, dtype=jnp.int32)
    phase = jnp.arange(part_count, dtype=jnp.int32)[:, None] * offsets[None, :] % seq_length
    angle = wrapped_angle(phase, seq_length, -2.0)
    real_part, imag_part = rotate(real_part, imag_part, angle[None, :, :, None])
    merged = jnp.concatenate([real_part, imag_part], axis=0).reshape(
        2 * field_count, row_count, chan_width
    )
    spread = regroup(merged)
    real_part = spread[:field_count]
    imag_part = spread[field_count:]
    cos_rows, sin_rows = unit_tables(row_count)
    spec_re = table_apply(cos_rows, real_part, "kb,fbc->fkc") + table_apply(
        sin_rows, imag_part, "kb,fbc->fkc"
    )
    spec_im = table_apply(cos_rows, imag_part, "kb,fbc->fkc") - table_apply(
        sin_rows, real_part, "kb,fbc->fkc"
    )
    return (spec_re, spec_im)


def inverse_transform(spec_re, spec_im):
    part_count = lax.axis_size("seq")
    position = lax.axis_index("seq")
    field_count, row_count, chan_width = spec_re.shape
    block_rows = row_count // part_count
    seq_length = row_count * part_count
    cos_rows, sin_rows = unit_tables(row_count)
    time_re = table_apply(cos_rows, spec_re, "bk,fkc->fbc") - table_apply(
        sin_rows, spec_im, "bk,fkc->fbc"
    )
    time_im = table_apply(cos_rows, spec_im, "bk,fkc->fbc") + table_apply(
        sin_rows, spec_re, "bk,fkc->fbc"
    )
    phase = position * jnp.arange(row_count, dtype=jnp.int32) % seq_length
    angle = wrapped_angle(phase, seq_length, 2.0)
    time_re, time_im = rotate(time_re, time_im, angle[None, :, None])
    merged = jnp.concatenate([time_re, time_im], axis=0)
    spread = regroup(merged).reshape(2 * field_count, part_count, block_rows, chan_width)
    cos_part, sin_part = unit_tables(part_count)
    result = table_apply(cos_part, spread[:field_count], "pk,fkbc->fpbc") - table_apply(
        sin_part, spread[field_count:], "pk,fkbc->fpbc"
    )
    settled = regroup(result.reshape(field_count, row_count, chan_width))
    return settled * (1.0 / seq_length)


def on_device(inputs, w_in, w_out, filt_fwd, filt_bwd, skip_gain, cotangent):
    input_rows = inputs[0]
    row_count, chan_width = input_rows.shape
    block_count = chan_width // BLOCK
    input_blocks = input_rows.reshape(row_count, block_count, BLOCK)
    w_blocks = w_in.reshape(block_count, BLOCK, 3, BLOCK)
    projected = jnp.einsum(
        "mni,nisj->smnj", input_blocks, w_blocks, preferred_element_type=jnp.float32
    )
    projected = projected.reshape(3, row_count, chan_width)
    keys, values, queries = (projected[0], projected[1], projected[2])
    mixed = keys * values
    spec_re, spec_im = forward_transform(jnp.stack([mixed, filt_fwd, filt_bwd]))
    mix_re, mix_im = (spec_re[0], spec_im[0])
    fwd_re, fwd_im = (spec_re[1], spec_im[1])
    bwd_re, bwd_im = (spec_re[2], spec_im[2])
    joint_re, joint_im = complex_product(fwd_re + bwd_re, fwd_im - bwd_im, mix_re, mix_im)
    long_conv = inverse_transform(joint_re[None], joint_im[None])[0]
    conv_out = long_conv + skip_gain * mixed
    gated = (queries * conv_out).astype(jnp.bfloat16)
    out_terms = jnp.dot(gated, w_out, preferred_element_type=jnp.float32)
    layer_out = lax.psum_scatter(out_terms, "chan", scatter_dimension=1, tiled=True).astype(
        jnp.bfloat16
    )
    grad_rows = cotangent[0]
    piece = lax.all_gather(grad_rows, "chan", axis=1, tiled=True)
    grad_gated = lax.dot_general(
        piece, w_out, (((1,), (1,)), ((), ())), preferred_element_type=jnp.float32
    )
    block_grad = lax.dot_general(
        gated, piece, (((0,), (0,)), ((), ())), preferred_element_type=jnp.float32
    )
    grad_wout = block_grad
    grad_gated, grad_wout = (grad_gated, grad_wout)
    grad_queries = grad_gated * conv_out
    grad_conv = grad_gated * queries
    grad_re, grad_im = forward_transform(grad_conv[None])
    grad_re, grad_im = (grad_re[0], grad_im[0])
    upper_re, upper_im = complex_product(fwd_re + bwd_re, bwd_im - fwd_im, grad_re, grad_im)
    cross_re, cross_im = complex_product(grad_re, grad_im, mix_re, -mix_im)
    results = inverse_transform(
        jnp.stack([upper_re, cross_re, cross_re]), jnp.stack([upper_im, cross_im, -cross_im])
    )
    back = results[0]
    grad_hfwd = results[-2]
    grad_hbwd = results[-1]
    grad_mixed = back + skip_gain * grad_conv
    grad_pre = jnp.stack([grad_mixed * values, grad_mixed * keys, grad_queries]).astype(
        jnp.bfloat16
    )
    pre_blocks = grad_pre.reshape(3, row_count, block_count, BLOCK)
    d_input = jnp.einsum("smnj,nisj->mni", pre_blocks, w_blocks, preferred_element_type=jnp.float32)
    d_input = d_input.reshape(row_count, chan_width).astype(jnp.bfloat16)
    grad_win = jnp.einsum(
        "mni,smnj->nisj", input_blocks, pre_blocks, preferred_element_type=jnp.float32
    )
    grad_win = grad_win.reshape(chan_width, 3 * BLOCK)
    grad_skip = jnp.sum(grad_conv * mixed, axis=0)
    grad_win, grad_wout, grad_skip = lax.psum((grad_win, grad_wout, grad_skip), ("seq", "rep"))
    grad_hfwd, grad_hbwd = lax.psum((grad_hfwd, grad_hbwd), "rep")
    scale = 1.0 / math.sqrt(lax.axis_size("rep") * lax.axis_size("seq") * row_count)
    return (
        layer_out[None],
        d_input[None],
        grad_win * scale,
        grad_wout * scale,
        grad_hfwd * scale,
        grad_hbwd * scale,
        grad_skip * scale,
    )


def solution(mesh):
    return jax.shard_map(
        on_device,
        mesh=mesh,
        in_specs=(
            P("rep", "seq", "chan"),
            P("chan", None),
            P("chan", None),
            P("seq", "chan"),
            P("seq", "chan"),
            P("chan"),
            P("rep", "seq", "chan"),
        ),
        out_specs=(
            P("rep", "seq", "chan"),
            P("rep", "seq", "chan"),
            P("chan", None),
            P("chan", None),
            P("seq", "chan"),
            P("seq", "chan"),
            P("chan"),
        ),
        check_vma=False,
    )
```

profile of v0, /device:TPU:6, one launch (start us, length us, event | category | flops | bytes accessed | tf_op | source)
XLA Modules:
  0.0 551.1 jit_solution(10543586648825998175)
XLA Ops:
  7.9 2.6 copy.79
  10.6 3.2 fusion.67
  13.8 22.4 %all-gather.3.cloned.1.call-done = bf16[1,256,2048]{2,1,0:T(8,128)(2,1)} async-done(((bf16[1,256,512]{2,1,0:T(8,128)(2,1)}), bf16[1,256,2048]{2,1,0:T(8,128)(2,1)}) %all-gather.3.cloned.1.call-update) | async-done | bytes 1048592 | tf_op jit(solution)/shard_map/all_gather | solution.py:125
  36.1 3.2 multiply_reduce_fusion
  40.4 5.9 %all-to-all-start.4 = ((f32[1,256,512]{2,0,1:T(1,128)}), f32[1,256,512]{2,0,1:T(1,128)S(1)}, u32[]{:S(2)}, u32[]{:S(2)}) async-start(f32[1,256,512]{2,0,1:T(1,128)} %copy.104), calls=%async_computation.5 | async-start | bytes 1048576 | tf_op jit(solution)/shard_map/all_to_all | solution.py:41
  53.1 2.9 copy.85
  56.0 5.7 %all-to-all-start = ((f32[3,256,512]{2,0,1:T(4,128)}), f32[3,256,512]{2,0,1:T(4,128)}, u32[]{:S(2)}, u32[]{:S(2)}) async-start(f32[3,256,512]{2,0,1:T(4,128)} %copy.85), calls=%async_computation | async-start | bytes 4194304 | tf_op jit(solution)/shard_map/all_to_all | solution.py:41
  66.5 21.9 %all-to-all-done = f32[3,256,512]{2,0,1:T(4,128)} async-done(((f32[3,256,512]{2,0,1:T(4,128)}), f32[3,256,512]{2,0,1:T(4,128)}, u32[]{:S(2)}, u32[]{:S(2)}) %all-to-all-start) | async-done | bytes 1572896 | tf_op jit(solution)/shard_map/all_to_all | solution.py:41
  88.4 6.1 %all-to-all-start.5 = ((f32[2,256,512]{2,0,1:T(2,128)}), f32[2,256,512]{2,0,1:T(2,128)}, u32[]{:S(2)}, u32[]{:S(2)}) async-start(f32[2,256,512]{2,0,1:T(2,128)} %copy.110), calls=%async_computation.6 | async-start | bytes 2097152 | tf_op jit(solution)/shard_map/all_to_all | solution.py:41
  96.6 2.5 fusion.9
  99.1 2.9 fusion
  104.4 3.9 copy.92
  109.8 6.0 %all-to-all-start.1 = ((f32[6,256,512]{2,0,1:T(8,128)}), f32[6,256,512]{2,0,1:T(8,128)}, u32[]{:S(2)}, u32[]{:S(2)}) async-start(f32[6,256,512]{2,0,1:T(8,128)} %copy.92), calls=%async_computation.1 | async-start | bytes 8388608 | tf_op jit(solution)/shard_map/all_to_all | solution.py:41
  115.8 2.4 fusion.281
  122.0 2.6 fusion.26
  124.7 40.2 %all-to-all-done.1 = f32[6,256,512]{2,0,1:T(8,128)} async-done(((f32[6,256,512]{2,0,1:T(8,128)}), f32[6,256,512]{2,0,1:T(8,128)}, u32[]{:S(2)}, u32[]{:S(2)}) %all-to-all-start.1) | async-done | bytes 3145760 | tf_op jit(solution)/shard_map/all_to_all | solution.py:41
  164.8 6.6 %fusion.279 = (f32[3,256,512]{2,0,1:T(4,128)}, f32[3,256,512]{2,0,1:T(4,128)}) fusion(f32[6,256,512]{2,0,1:T(8,128)} %all-to-all-done.1), kind=kLoop, calls=%fused_computation.333 | loop fusion | bytes 6291456 | tf_op jit(solution)/shard_map/slice | solution.py:62
  171.4 2.7 copy.133
  174.1 2.9 copy.134
  177.0 4.0 fusion.63
  181.0 2.4 fusion.65
  183.4 2.5 subtract_bitcast_fusion.2
  186.0 2.5 add_bitcast_fusion.1
  188.5 3.8 fusion.277
  203.3 5.8 %all-to-all-start.2 = ((f32[2,256,512]{2,0,1:T(2,128)}), f32[2,256,512]{2,0,1:T(2,128)}, u32[]{:S(2)}, u32[]{:S(2)}) async-start(f32[2,256,512]{2,0,1:T(2,128)} %copy.95), calls=%async_computation.2 | async-start | bytes 2097152 | tf_op jit(solution)/shard_map/all_to_all | solution.py:41
  209.1 3.9 fusion.11
  213.0 2.4 fusion.20
  215.5 2.5 convolution_add_fusion
  218.0 2.7 subtract_bitcast_fusion.1
  222.6 5.2 copy.111
  227.7 5.8 %all-to-all-start.6 = ((f32[6,256,512]{2,0,1:T(8,128)}), f32[6,256,512]{2,0,1:T(8,128)}, u32[]{:S(2)}, u32[]{:S(2)}) async-start(f32[6,256,512]{2,0,1:T(8,128)} %copy.111), calls=%async_computation.7 | async-start | bytes 8388608 | tf_op jit(solution)/shard_map/all_to_all | solution.py:41
  233.5 2.4 fusion.280
  239.5 43.2 %all-to-all-done.6 = f32[6,256,512]{2,0,1:T(8,128)} async-done(((f32[6,256,512]{2,0,1:T(8,128)}), f32[6,256,512]{2,0,1:T(8,128)}, u32[]{:S(2)}, u32[]{:S(2)}) %all-to-all-start.6) | async-done | bytes 3145760 | tf_op jit(solution)/shard_map/all_to_all | solution.py:41
  282.7 5.0 all-to-all-start.3
  287.7 4.5 fusion.278
  292.7 2.5 fusion.2
  295.7 2.6 subtract_bitcast_fusion
  301.6 5.8 %all-to-all-start.7 = ((f32[3,256,512]{2,0,1:T(4,128)}), f32[3,256,512]{2,0,1:T(4,128)}, u32[]{:S(2)}, u32[]{:S(2)}) async-start(f32[3,256,512]{2,0,1:T(4,128)} %copy.117), calls=%async_computation.8 | async-start | bytes 4194304 | tf_op jit(solution)/shard_map/all_to_all | solution.py:41
  308.6 25.5 %all-to-all-done.7 = f32[3,256,512]{2,0,1:T(4,128)} async-done(((f32[3,256,512]{2,0,1:T(4,128)}), f32[3,256,512]{2,0,1:T(4,128)}, u32[]{:S(2)}, u32[]{:S(2)}) %all-to-all-start.7) | async-done | bytes 1572896 | tf_op jit(solution)/shard_map/all_to_all | solution.py:41
  334.1 2.7 copy.118
  346.1 2.7 fusion.21
  351.3 63.1 %psum.39 = f32[512]{0:T(512)S(1)} all-reduce(f32[512]{0:T(512)S(1)} %get-tuple-element.32), channel_id=1, replica_groups=mesh['seq'=16,'chan'=4,'rep'=2] {'seq','rep'}, use_global_device_ids=true, to_apply=%region_6.7 | all-reduce | flops 512 | bytes 4096 | tf_op jit(solution)/shard_map/psum | solution.py:158
  414.9 2.8 fusion.19
  420.9 90.7 %all-reduce.5.cloned.1.call-done = (f32[512,1536]{0,1:T(8,128)}, f32[512,2048]{1,0:T(8,128)}) async-done(((f32[512,1536]{0,1:T(8,128)}, f32[512,2048]{1,0:T(8,128)}), (f32[512,1536]{0,1:T(8,128)}, f32[512,2048]{1,0:T(8,128)})) %all-reduce.5.cloned.1.call-update) | async-done | bytes 7340048 | tf_op jit(solution)/shard_map/psum | solution.py:158
  511.6 3.9 broadcast_multiply_fusion.1
  515.5 3.5 copy.122
  519.1 5.0 broadcast_multiply_fusion
  524.0 18.3 %reduce-scatter.2.cloned.1.call-done = f32[256,512]{1,0:T(8,128)} async-done(((f32[256,2048]{1,0:T(8,128)}), f32[256,512]{1,0:T(8,128)}) %reduce-scatter.2.cloned.1.call-update) | async-done | bytes 524304 | tf_op jit(solution)/shard_map/reduce_scatter | solution.py:121
  (114 shorter events, 62.3 us)
Async XLA Ops:
  7.2 28.9 %copy-start = (bf16[512,2048]{1,0:T(8,128)(2,1)S(1)}, bf16[512,2048]{1,0:T(8,128)(2,1)}, u32[]{:S(2)}) copy-start(bf16[512,2048]{1,0:T(8,128)(2,1)} %param.9) | copy-start | bytes 6291460
  7.2 28.9 %all-gather.3.cloned.1.call-start = ((), (), s32[]{:S(2)}) async-start(), calls=%async_computation.10 | async-start | bytes 1310720 | tf_op jit(solution)/shard_map/all_gather | solution.py:125
  7.9 2.7 copy-start.19
  40.4 15.6 %all-to-all-start.4 = ((f32[1,256,512]{2,0,1:T(1,128)}), f32[1,256,512]{2,0,1:T(1,128)S(1)}, u32[]{:S(2)}, u32[]{:S(2)}) async-start(f32[1,256,512]{2,0,1:T(1,128)} %copy.104), calls=%async_computation.5 | async-start | bytes 1048576 | tf_op jit(solution)/shard_map/all_to_all | solution.py:41
  50.3 1.4 copy-start.5
  50.3 1.5 copy-start.6
  56.0 32.4 %all-to-all-start = ((f32[3,256,512]{2,0,1:T(4,128)}), f32[3,256,512]{2,0,1:T(4,128)}, u32[]{:S(2)}, u32[]{:S(2)}) async-start(f32[3,256,512]{2,0,1:T(4,128)} %copy.85), calls=%async_computation | async-start | bytes 4194304 | tf_op jit(solution)/shard_map/all_to_all | solution.py:41
  88.4 21.4 %all-to-all-start.5 = ((f32[2,256,512]{2,0,1:T(2,128)}), f32[2,256,512]{2,0,1:T(2,128)}, u32[]{:S(2)}, u32[]{:S(2)}) async-start(f32[2,256,512]{2,0,1:T(2,128)} %copy.110), calls=%async_computation.6 | async-start | bytes 2097152 | tf_op jit(solution)/shard_map/all_to_all | solution.py:41
  109.8 55.0 %all-to-all-start.1 = ((f32[6,256,512]{2,0,1:T(8,128)}), f32[6,256,512]{2,0,1:T(8,128)}, u32[]{:S(2)}, u32[]{:S(2)}) async-start(f32[6,256,512]{2,0,1:T(8,128)} %copy.92), calls=%async_computation.1 | async-start | bytes 8388608 | tf_op jit(solution)/shard_map/all_to_all | solution.py:41
  118.3 3.7 copy-start.11
  122.0 66.4 %copy-start.10 = (f32[1,256,512]{1,2,0:T(8,128)}, f32[1,256,512]{1,2,0:T(8,128)S(1)}, u32[]{:S(2)}) copy-start(f32[1,256,512]{1,2,0:T(8,128)S(1)} %fusion.15) | copy-start | bytes 1572868
  177.0 4.0 copy-start.1
  183.4 2.5 copy-start.2
  185.9 2.5 copy-start.12
  186.0 2.5 copy-start.22
  203.3 24.4 %all-to-all-start.2 = ((f32[2,256,512]{2,0,1:T(2,128)}), f32[2,256,512]{2,0,1:T(2,128)}, u32[]{:S(2)}, u32[]{:S(2)}) async-start(f32[2,256,512]{2,0,1:T(2,128)} %copy.95), calls=%async_computation.2 | async-start | bytes 2097152 | tf_op jit(solution)/shard_map/all_to_all | solution.py:41
  209.1 3.9 copy-start.8
  209.1 3.9 copy-start.9
  213.0 2.5 copy-start.13
  213.0 2.5 copy-start.14
  227.7 55.0 %all-to-all-start.6 = ((f32[6,256,512]{2,0,1:T(8,128)}), f32[6,256,512]{2,0,1:T(8,128)}, u32[]{:S(2)}, u32[]{:S(2)}) async-start(f32[6,256,512]{2,0,1:T(8,128)} %copy.111), calls=%async_computation.7 | async-start | bytes 8388608 | tf_op jit(solution)/shard_map/all_to_all | solution.py:41
  282.7 18.9 %all-to-all-start.3 = ((f32[1,256,512]{2,0,1:T(1,128)}), f32[1,256,512]{2,0,1:T(1,128)S(1)}, u32[]{:S(2)}, u32[]{:S(2)}) async-start(f32[1,256,512]{2,0,1:T(1,128)} %copy.101), calls=%async_computation.3 | async-start | bytes 1048576 | tf_op jit(solution)/shard_map/all_to_all | solution.py:41
  301.6 32.5 %all-to-all-start.7 = ((f32[3,256,512]{2,0,1:T(4,128)}), f32[3,256,512]{2,0,1:T(4,128)}, u32[]{:S(2)}, u32[]{:S(2)}) async-start(f32[3,256,512]{2,0,1:T(4,128)} %copy.117), calls=%async_computation.8 | async-start | bytes 4194304 | tf_op jit(solution)/shard_map/all_to_all | solution.py:41
  307.4 110.3 %all-reduce.7.cloned.1.call-start = ((), (), s32[]{:S(2)}) async-start(), calls=%async_computation.12 | async-start | bytes 2097152 | tf_op jit(solution)/shard_map/psum | solution.py:159
  338.3 1.1 copy-start.3
  339.4 1.2 copy-start.7
  339.4 1.2 copy-start.23
  340.6 171.0 %all-reduce.5.cloned.1.call-start = ((), (), s32[]{:S(2)}) async-start(), calls=%async_computation.11 | async-start | bytes 14680064 | tf_op jit(solution)/shard_map/psum | solution.py:158
  342.4 3.7 copy-start.15
  342.4 3.6 copy-start.17
  342.4 1.4 copy-start.20
  343.8 2.3 copy-start.4
  348.8 193.5 %reduce-scatter.2.cloned.1.call-start = ((), (), s32[]{:S(2)}) async-start(), calls=%async_computation.9 | async-start | bytes 2621440 | tf_op jit(solution)/shard_map/reduce_scatter | solution.py:121
  351.3 63.7 %copy-start.16 = (bf16[1,256,512]{1,2,0:T(8,128)(2,1)S(1)}, bf16[1,256,512]{1,2,0:T(8,128)(2,1)}, u32[]{:S(2)}) copy-start(bf16[1,256,512]{1,2,0:T(8,128)(2,1)} %copy-done.15) | copy-start | bytes 786436
  351.3 63.7 %copy-start.18 = (bf16[1,256,512]{1,2,0:T(8,128)(2,1)S(1)}, bf16[1,256,512]{1,2,0:T(8,128)(2,1)}, u32[]{:S(2)}) copy-start(bf16[1,256,512]{1,2,0:T(8,128)(2,1)} %copy-done.17) | copy-start | bytes 786436
  417.7 2.2 copy-start.21
Sparse Core Ops, SparseCore 0:
  9.7 26.4 all-gather.2
  340.7 46.6 all-reduce.6
  391.5 120.0 all-reduce.4
  513.8 28.4 reduce-scatter.1
where the time goes:
time: 559 us; the launch traced here: 551 us
  waiting for transfers between devices  264 us (47%)
  matrix products  69.8 us (12%)
  local copies, waits for them, and re-layouts  68 us (12%)
  blocking collectives  63.1 us (11%)
  starting transfers between devices  46.3 us (8%)
  other arithmetic  24.7 us (4%)
  between operations  14.8 us (3%)
    all_to_all x8, waiting for transfers between devices, regroup(): lax.all_to_all(stacked, 'seq', split_axis=1, concat_axis=1, tiled=True)  132 us
    psum x1, waiting for transfers between devices, on_device(): lax.psum((grad_win, grad_wout, grad_skip), ('seq', 'rep'))  90.7 us
    psum x1, blocking collectives, on_device(): lax.psum((grad_win, grad_wout, grad_skip), ('seq', 'rep'))  63.1 us
    dot_general x24, matrix products, table_apply(): return jnp.einsum(form, table, fields, precision=HIGHEST_PRECISION)  53.6 us
    all_to_all x8, starting transfers between devices, regroup(): lax.all_to_all(stacked, 'seq', split_axis=1, concat_axis=1, tiled=True)  45.9 us
    all_gather x1, waiting for transfers between devices, on_device(): piece = lax.all_gather(grad_rows, 'chan', axis=1, tiled=True)  22.4 us
    unnamed x61, local copies, waits for them, and re-layouts  20.4 us
    reduce_scatter x1, waiting for transfers between devices, on_device(): lax.psum_scatter(out_terms, 'chan', scatter_dimension=1, tiled=True)  18.3 us
  transfers between devices with their start and end apart: 12, of which 8 were waited for; matrix products, arithmetic and copies ran while one was open for 20% of the time, Pallas kernels for 0%

commit v1 on v0

v1 whole, which is shorter than its diff:
```python
import math

import jax
import jax.numpy as jnp
import numpy as np
from jax import lax
from jax.sharding import PartitionSpec as P

BLOCK = 512

HIGHEST_PRECISION = lax.Precision.HIGHEST


def factor_split(length):
    first = 1 << (int(math.log2(length)) // 2)
    return first, length // first


def unit_table(size):
    index_row = np.arange(size)
    angle = 2.0 * np.pi * ((index_row[:, None] * index_row[None, :]) % size) / size
    return (jnp.asarray(np.cos(angle), jnp.float32), jnp.asarray(np.sin(angle), jnp.float32))


def twiddle_table(rows, cols):
    length = rows * cols
    phase = (np.arange(rows)[:, None] * np.arange(cols)[None, :]) % length
    angle = 2.0 * np.pi * phase / length
    return (jnp.asarray(np.cos(angle), jnp.float32), jnp.asarray(np.sin(angle), jnp.float32))


def table_apply(table, fields, form):
    return jnp.einsum(form, table, fields, precision=HIGHEST_PRECISION)


def real_spectrum(signal):
    field_count, length, width = signal.shape
    first, second = factor_split(length)
    grid = signal.reshape(field_count, first, second, width)
    cos_a, sin_a = unit_table(first)
    cos_b, sin_b = unit_table(second)
    cos_t, sin_t = twiddle_table(first, second)
    y_re = table_apply(cos_a, grid, "kn,fnmc->fkmc")
    y_im = -table_apply(sin_a, grid, "kn,fnmc->fkmc")
    cos_t = cos_t[None, :, :, None]
    sin_t = sin_t[None, :, :, None]
    z_re = y_re * cos_t + y_im * sin_t
    z_im = y_im * cos_t - y_re * sin_t
    x_re = table_apply(cos_b, z_re, "jm,fkmc->fjkc") + table_apply(sin_b, z_im, "jm,fkmc->fjkc")
    x_im = table_apply(cos_b, z_im, "jm,fkmc->fjkc") - table_apply(sin_b, z_re, "jm,fkmc->fjkc")
    return x_re, x_im


def real_inverse(spec_re, spec_im):
    field_count, second, first, width = spec_re.shape
    length = first * second
    cos_a, sin_a = unit_table(first)
    cos_b, sin_b = unit_table(second)
    cos_t, sin_t = twiddle_table(first, second)
    a_re = table_apply(cos_b, spec_re, "mj,fjkc->fmkc") - table_apply(sin_b, spec_im, "mj,fjkc->fmkc")
    a_im = table_apply(cos_b, spec_im, "mj,fjkc->fmkc") + table_apply(sin_b, spec_re, "mj,fjkc->fmkc")
    cos_t = cos_t.T[None, :, :, None]
    sin_t = sin_t.T[None, :, :, None]
    b_re = a_re * cos_t - a_im * sin_t
    b_im = a_re * sin_t + a_im * cos_t
    out = table_apply(cos_a, b_re, "nk,fmkc->fnmc") - table_apply(sin_a, b_im, "nk,fmkc->fnmc")
    return out.reshape(field_count, length, width) * (1.0 / length)


def lag_reverse(signal, axis):
    return jnp.roll(jnp.flip(signal, axis=axis), 1, axis=axis)


def complex_product(left_re, left_im, right_re, right_im):
    return (left_re * right_re - left_im * right_im, left_re * right_im + left_im * right_re)


def to_channels(fields):
    return lax.all_to_all(fields, "seq", split_axis=2, concat_axis=1, tiled=True)


def to_rows(fields):
    return lax.all_to_all(fields, "seq", split_axis=1, concat_axis=2, tiled=True)


def on_device(inputs, w_in, w_out, filt_fwd, filt_bwd, skip_gain, cotangent):
    input_rows = inputs[0]
    row_count, chan_width = input_rows.shape
    block_count = chan_width // BLOCK
    input_blocks = input_rows.reshape(row_count, block_count, BLOCK)
    w_blocks = w_in.reshape(block_count, BLOCK, 3, BLOCK)
    grad_rows = cotangent[0]
    piece = lax.all_gather(grad_rows, "chan", axis=1, tiled=True)
    projected = jnp.einsum(
        "mni,nisj->smnj", input_blocks, w_blocks, preferred_element_type=jnp.float32
    )
    projected = projected.reshape(3, row_count, chan_width)
    keys, values, queries = (projected[0], projected[1], projected[2])
    mixed = keys * values
    spread = to_channels(jnp.stack([mixed, filt_fwd, filt_bwd]))
    mixed_cs = spread[0]
    joint_filter = spread[1] + lag_reverse(spread[2], 0)
    spec_re, spec_im = real_spectrum(jnp.stack([mixed_cs, joint_filter]))
    mix_re, mix_im = (spec_re[0], spec_im[0])
    gain_re, gain_im = (spec_re[1], spec_im[1])
    joint_re, joint_im = complex_product(gain_re, gain_im, mix_re, mix_im)
    long_conv = to_rows(real_inverse(joint_re[None], joint_im[None]))[0]
    conv_out = long_conv + skip_gain * mixed
    gated = (queries * conv_out).astype(jnp.bfloat16)
    out_terms = jnp.dot(gated, w_out, preferred_element_type=jnp.float32)
    layer_out = lax.psum_scatter(out_terms, "chan", scatter_dimension=1, tiled=True).astype(
        jnp.bfloat16
    )
    grad_gated = lax.dot_general(
        piece, w_out, (((1,), (1,)), ((), ())), preferred_element_type=jnp.float32
    )
    grad_wout = lax.dot_general(
        gated, piece, (((0,), (0,)), ((), ())), preferred_element_type=jnp.float32
    )
    grad_wout = lax.psum(grad_wout, ("seq", "rep"))
    grad_queries = grad_gated * conv_out
    grad_conv = grad_gated * queries
    grad_cs = to_channels(grad_conv[None])
    grad_re, grad_im = real_spectrum(grad_cs)
    grad_re, grad_im = (grad_re[0], grad_im[0])
    back_re, back_im = complex_product(gain_re, -gain_im, grad_re, grad_im)
    cross_re, cross_im = complex_product(grad_re, grad_im, mix_re, -mix_im)
    results = real_inverse(jnp.stack([back_re, cross_re]), jnp.stack([back_im, cross_im]))
    back = to_rows(results[0][None])[0]
    grad_hfwd = lax.psum(results[1], "rep")
    grad_hbwd = lag_reverse(grad_hfwd, 0)
    filt_grads = to_rows(jnp.stack([grad_hfwd, grad_hbwd]))
    grad_mixed = back + skip_gain * grad_conv
    grad_pre = jnp.stack([grad_mixed * values, grad_mixed * keys, grad_queries]).astype(
        jnp.bfloat16
    )
    pre_blocks = grad_pre.reshape(3, row_count, block_count, BLOCK)
    d_input = jnp.einsum("smnj,nisj->mni", pre_blocks, w_blocks, preferred_element_type=jnp.float32)
    d_input = d_input.reshape(row_count, chan_width).astype(jnp.bfloat16)
    grad_win = jnp.einsum(
        "mni,smnj->nisj", input_blocks, pre_blocks, preferred_element_type=jnp.float32
    )
    grad_win = grad_win.reshape(chan_width, 3 * BLOCK)
    grad_skip = jnp.sum(grad_conv * mixed, axis=0)
    grad_win, grad_skip = lax.psum((grad_win, grad_skip), ("seq", "rep"))
    scale = 1.0 / math.sqrt(lax.axis_size("rep") * lax.axis_size("seq") * row_count)
    return (
        layer_out[None],
        d_input[None],
        grad_win * scale,
        grad_wout * scale,
        filt_grads[0] * scale,
        filt_grads[1] * scale,
        grad_skip * scale,
    )


def solution(mesh):
    return jax.shard_map(
        on_device,
        mesh=mesh,
        in_specs=(
            P("rep", "seq", "chan"),
            P("chan", None),
            P("chan", None),
            P("seq", "chan"),
            P("seq", "chan"),
            P("chan"),
            P("rep", "seq", "chan"),
        ),
        out_specs=(
            P("rep", "seq", "chan"),
            P("rep", "seq", "chan"),
            P("chan", None),
            P("chan", None),
            P("seq", "chan"),
            P("seq", "chan"),
            P("chan"),
        ),
        check_vma=False,
    )
```

time: 559 us -> 434 us (0.78)
  waiting for transfers between devices: 264 us -> 70.9 us
  other arithmetic: 24.7 us -> 68.9 us
  local copies, waits for them, and re-layouts: 68 us -> 92.2 us
  starting transfers between devices: 46.3 us -> 29.8 us
  blocking collectives: 63.1 us -> 73.1 us
  matrix products: 69.8 us -> 77.9 us
    all_to_all x8 -> x5, waiting for transfers between devices: 132 us -> 26 us  [the longest x2 26 us: to_channels(): lax.all_to_all(fields, 'seq', split_axis=2, concat_axis=1, tiled=True)]
    psum x2, waiting for transfers between devices: 90.7 us -> 25.9 us  [the longest x1 21.2 us: on_device(): grad_win, grad_skip = lax.psum((grad_win, grad_skip), ('seq', 'rep'))]
    unnamed x0 -> x2, other arithmetic: none -> 40.6 us
    unnamed x61 -> x75, local copies, waits for them, and re-layouts: 20.4 us -> 45.9 us
    all_gather x1, waiting for transfers between devices: 22.4 us -> 0.01 us  [on_device(): piece = lax.all_gather(grad_rows, 'chan', axis=1, tiled=True)]
    all_to_all x8 -> x5, starting transfers between devices: 45.9 us -> 29.4 us  [the longest x3 18 us: to_rows(): lax.all_to_all(fields, 'seq', split_axis=1, concat_axis=2, tiled=True)]
    all_to_all x0 -> x3, other arithmetic: none -> 10.1 us  [to_rows(): lax.all_to_all(fields, 'seq', split_axis=1, concat_axis=2, tiled=True)]
    psum x1, blocking collectives: 63.1 us -> 73.1 us  [on_device(): grad_win, grad_skip = lax.psum((grad_win, grad_skip), ('seq', 'rep'))]
  transfers between devices with their start and end apart: 12 -> 9, of which waited for: 8 -> 4; matrix products, arithmetic and copies ran while one was open for 20% -> 38% of each run, Pallas kernels for 0% -> 0%
where the time goes in v1:
time: 434 us; the launch traced here: 427 us
  local copies, waits for them, and re-layouts  92.2 us (21%)
  matrix products  77.9 us (18%)
  blocking collectives  73.1 us (17%)
  waiting for transfers between devices  70.9 us (16%)
  other arithmetic  68.9 us (16%)
  starting transfers between devices  29.8 us (7%)
  between operations  14.7 us (3%)
    psum x1, blocking collectives, on_device(): grad_win, grad_skip = lax.psum((grad_win, grad_skip), ('seq', 'rep'))  73.1 us
    dot_general x24, matrix products, table_apply(): return jnp.einsum(form, table, fields, precision=HIGHEST_PRECISION)  62.9 us
    unnamed x75, local copies, waits for them, and re-layouts  45.9 us
    unnamed x2, other arithmetic  40.6 us
    all_to_all x2, waiting for transfers between devices, to_channels(): lax.all_to_all(fields, 'seq', split_axis=2, concat_axis=1, tiled=True)  26 us
    psum x1, waiting for transfers between devices, on_device(): grad_win, grad_skip = lax.psum((grad_win, grad_skip), ('seq', 'rep'))  21.2 us
    reduce_scatter x1, waiting for transfers between devices, on_device(): lax.psum_scatter(out_terms, 'chan', scatter_dimension=1, tiled=True)  18.3 us
    all_to_all x3, starting transfers between devices, to_rows(): lax.all_to_all(fields, 'seq', split_axis=1, concat_axis=2, tiled=True)  18 us
  transfers between devices with their start and end apart: 9, of which 4 were waited for; matrix products, arithmetic and copies ran while one was open for 38% of the time, Pallas kernels for 0%

profile of v1, /device:TPU:6, one launch (start us, length us, event | category | flops | bytes accessed | tf_op | source)
XLA Modules:
  0.0 427.4 jit_solution(14961464643709578261)
XLA Ops:
  7.2 2.8 copy.142
  14.8 2.4 copy.148
  17.2 6.8 %all-to-all-start = ((f32[3,256,512]{1,0,2:T(4,128)}), f32[3,256,512]{1,0,2:T(4,128)}, u32[]{:S(2)}, u32[]{:S(2)}) async-start(f32[3,256,512]{1,0,2:T(4,128)} %copy.148), calls=%async_computation | async-start | bytes 4194304 | tf_op jit(solution)/shard_map/all_to_all | solution.py:79
  24.7 26.0 %all-to-all-done = f32[3,256,512]{1,0,2:T(4,128)} async-done(((f32[3,256,512]{1,0,2:T(4,128)}), f32[3,256,512]{1,0,2:T(4,128)}, u32[]{:S(2)}, u32[]{:S(2)}) %all-to-all-start) | async-done | bytes 1572896 | tf_op jit(solution)/shard_map/all_to_all | solution.py:79
  50.7 2.5 copy.219
  54.8 2.5 reverse.4
  73.2 3.6 fusion.56
  76.7 5.2 %subtract_bitcast_fusion = f32[2,64,64,32]{1,2,3,0:T(8,128)} fusion(f32[2,64,32,64]{3,1,2,0:T(8,128)S(1)} %fusion.56, f32[64,64,1,1]{1,0,3,2:T(8,128)S(1)} %copy-done.18, f32[2,64,32,64]{3,1,2,0:T(8,128)S(1)} %fusion.13, f32[2,64,32,64]{3,1,2,0:T(8,128)S(1)} %fusion.12, f32[64,64]{0,1:T(8,128)S(1)} %copy-done.8, f32[64,64]{0,1:T(8,128)S(1)} %copy-done.9), kind=kOutput, calls=%fused_computation.20 | convolution fusion | flops 202637312 | bytes 4243456 | tf_op jit(solution)/shard_map/jm,fkmc->fjkc/dot_general | solution.py:33
  82.0 3.2 multiply_reduce_fusion
  87.4 4.7 %all-to-all-start.2 = ((f32[1,256,512]{1,0,2:T(1,128)}), f32[1,256,512]{1,0,2:T(1,128)S(1)}, u32[]{:S(2)}, u32[]{:S(2)}) async-start(f32[1,256,512]{1,0,2:T(1,128)} %copy.165), calls=%async_computation.3 | async-start | bytes 1048576 | tf_op jit(solution)/shard_map/all_to_all | solution.py:79
  92.1 5.4 %fusion.60 = f32[2,64,32,64]{3,1,2,0:T(8,128)S(1)} fusion(f32[64,64,1,1]{1,0,3,2:T(8,128)S(1)} %copy-done.17, f32[2,64,32,64]{3,1,2,0:T(8,128)} %copy-done.1, f32[2,64,32,64]{3,1,2,0:T(8,128)} %copy-done.3, f32[64,64]{0,1:T(8,128)S(1)} %copy-done.8, f32[64,64]{0,1:T(8,128)S(1)} %copy-done.9), kind=kOutput, calls=%fused_computation.90 | convolution fusion | flops 202375168 | bytes 3194880 | tf_op jit(solution)/shard_map/jm,fkmc->fjkc/dot_general | solution.py:33
  97.5 4.8 %add_bitcast_fusion = f32[2,64,64,32]{1,2,3,0:T(8,128)} fusion(f32[2,64,32,64]{3,1,2,0:T(8,128)S(1)} %fusion.60, f32[64,64,1,1]{1,0,3,2:T(8,128)S(1)} %copy-done.18, f32[2,64,32,64]{3,1,2,0:T(8,128)S(1)} %copy-done.2, f32[2,64,32,64]{3,1,2,0:T(8,128)S(1)} %copy-done.4, f32[64,64]{0,1:T(8,128)S(1)} %copy-done.8, f32[64,64]{0,1:T(8,128)S(1)} %copy-done.9), kind=kOutput, calls=%fused_computation.21 | convolution fusion | flops 202637312 | bytes 4243456 | tf_op jit(solution)/shard_map/jm,fkmc->fjkc/dot_general | solution.py:33
  114.2 3.2 multiply_subtract_fusion.1
  117.4 3.1 fusion.8
  120.5 3.1 fusion.9
  129.6 2.8 fusion.22
  132.4 4.1 copy.209
  136.9 20.3 %reduce = f32[4096,32]{1,0:T(8,128)} reduce(f32[4096,1,32]{2,1,0:T(1,128)} %bitcast.310, f32[]{:T(128)} %broadcast.40), dimensions={1}, to_apply=%bitcast.249.reduce_sub_computation | reduce | bytes 1048580
  157.2 3.1 reshape.238
  160.3 6.2 %all-to-all-start.1 = ((f32[16,1,8192]{2,1,0:T(1,128)}), f32[16,1,8192]{2,1,0:T(1,128)}, u32[]{:S(2)}, u32[]{:S(2)}) async-start(f32[16,1,8192]{2,1,0:T(1,128)} %reshape.238), calls=%async_computation.1 | async-start | bytes 1048576 | tf_op jit(solution)/shard_map/all_to_all | solution.py:83
  166.6 3.9 fusion.15
  172.4 3.5 fusion.1
  175.9 3.6 multiply_bitcast_fusion
  180.6 3.1 copy.211
  183.7 20.3 %reduce.2 = f32[4096,32]{1,0:T(8,128)} reduce(f32[4096,1,32]{2,1,0:T(1,128)} %bitcast.311, f32[]{:T(128)} %broadcast.40), dimensions={1}, to_apply=%bitcast.251.reduce_sub_computation | reduce | bytes 1048580
  204.0 3.1 reshape.240
  207.1 5.7 %all-to-all-start.3 = ((f32[16,1,8192]{2,1,0:T(1,128)}), f32[16,1,8192]{2,1,0:T(1,128)}, u32[]{:S(2)}, u32[]{:S(2)}) async-start(f32[16,1,8192]{2,1,0:T(1,128)} %reshape.240), calls=%async_computation.4 | async-start | bytes 1048576 | tf_op jit(solution)/shard_map/all_to_all | solution.py:83
  215.6 2.9 reduce.1
  218.5 4.8 %reshape.239 = f32[4096,1,32]{2,1,0:T(1,128)} reshape(f32[16,8192]{1,0:T(8,128)S(1)} %reduce.1) | data formatting | bytes 1048576
  226.7 2.9 reduce.3
  229.6 4.8 %reshape.241 = f32[4096,1,32]{2,1,0:T(1,128)} reshape(f32[16,8192]{1,0:T(8,128)S(1)} %reduce.3) | data formatting | bytes 1048576
  234.4 2.3 copy.212
  242.4 2.7 fusion.33
  247.6 4.7 %all-reduce.4.cloned.1.call-done = f32[4096,32]{0,1:T(8,128)} async-done(((f32[4096,32]{0,1:T(8,128)}), f32[4096,32]{0,1:T(8,128)}) %all-reduce.4.cloned.1.call-update) | async-done | bytes 524304 | tf_op jit(solution)/shard_map/psum | solution.py:130
  253.5 2.3 reverse.5
  257.0 4.4 %copy.183 = f32[2,4096,32]{2,0,1:T(2,128)} copy(f32[2,4096,32]{1,2,0:T(8,128)S(1)} %pad_maximum_fusion.14) | data formatting | bytes 2097152 | tf_op jit(solution)/shard_map/stack | solution.py:132
  261.4 6.5 %reshape.242 = f32[16,1,16384]{2,1,0:T(1,128)} reshape(f32[4096,2,32]{2,1,0:T(2,128)} %bitcast.306) | data formatting | bytes 2097152
  267.9 6.0 %all-to-all-start.4 = ((f32[16,1,16384]{2,1,0:T(1,128)}), f32[16,1,16384]{2,1,0:T(1,128)}, u32[]{:S(2)}, u32[]{:S(2)}) async-start(f32[16,1,16384]{2,1,0:T(1,128)} %reshape.242), calls=%async_computation.5 | async-start | bytes 2097152 | tf_op jit(solution)/shard_map/all_to_all | solution.py:83
  274.0 73.1 %psum.31 = f32[512]{0:T(512)S(1)} all-reduce(f32[512]{0:T(512)S(1)} %get-tuple-element.37), channel_id=1, replica_groups=mesh['seq'=16,'chan'=4,'rep'=2] {'seq','rep'}, use_global_device_ids=true, to_apply=%region_5.6 | all-reduce | flops 512 | bytes 4096 | tf_op jit(solution)/shard_map/psum | solution.py:145
  347.6 2.7 fusion.26
  350.3 4.3 %reduce.4 = f32[16,16384]{1,0:T(8,128)S(1)} reduce(f32[16,1,16384]{2,1,0:T(1,128)} %all-to-all-done.4, f32[]{:T(128)} %broadcast.40), dimensions={1}, to_apply=%all_to_all.67.reduce_sub_computation | reduce | bytes 2097156 | tf_op jit(solution)/shard_map/all_to_all | solution.py:83
  354.7 4.9 %reshape.243 = f32[4096,2,32]{2,1,0:T(2,128)} reshape(f32[16,16384]{1,0:T(8,128)S(1)} %reduce.4) | data formatting | bytes 2097152
  359.6 3.8 copy.213
  366.9 21.2 %all-reduce.6.cloned.1.call-done = (f32[512,1536]{0,1:T(8,128)}, f32[512,2048]{1,0:T(8,128)}) async-done(((f32[512,1536]{0,1:T(8,128)}, f32[512,2048]{1,0:T(8,128)}), (f32[512,1536]{0,1:T(8,128)}, f32[512,2048]{1,0:T(8,128)})) %all-reduce.6.cloned.1.call-update) | async-done | bytes 7340048 | tf_op jit(solution)/shard_map/psum | solution.py:145
  388.1 3.9 broadcast_multiply_fusion.1
  392.1 3.5 copy.187
  395.6 5.0 %broadcast_multiply_fusion = f32[512,2048]{1,0:T(8,128)} fusion(f32[512,2048]{1,0:T(8,128)} %get-tuple-element.36), kind=kLoop, calls=%fused_computation.18 | loop fusion | flops 1048576 | bytes 8388608 | tf_op jit(solution)/shard_map/mul | solution.py:151
  400.6 18.3 %reduce-scatter.2.cloned.1.call-done = f32[256,512]{1,0:T(8,128)} async-done(((f32[256,2048]{1,0:T(8,128)}), f32[256,512]{1,0:T(8,128)}) %reduce-scatter.2.cloned.1.call-update) | async-done | bytes 524304 | tf_op jit(solution)/shard_map/reduce_scatter | solution.py:111
  (130 shorter events, 68.7 us)
Async XLA Ops:
  7.2 74.8 %copy-start = (bf16[512,2048]{1,0:T(8,128)(2,1)S(1)}, bf16[512,2048]{1,0:T(8,128)(2,1)}, u32[]{:S(2)}) copy-start(bf16[512,2048]{1,0:T(8,128)(2,1)} %param.33) | copy-start | bytes 6291460
  7.2 2.8 copy-start.27
  7.2 4.2 copy-start.25
  13.4 1.2 copy-start.5
  17.2 33.5 %all-to-all-start = ((f32[3,256,512]{1,0,2:T(4,128)}), f32[3,256,512]{1,0,2:T(4,128)}, u32[]{:S(2)}, u32[]{:S(2)}) async-start(f32[3,256,512]{1,0,2:T(4,128)} %copy.148), calls=%async_computation | async-start | bytes 4194304 | tf_op jit(solution)/shard_map/all_to_all | solution.py:79
  24.0 58.0 %all-gather.3.cloned.1.call-start = ((), (), s32[]{:S(2)}) async-start(), calls=%async_computation.8 | async-start | bytes 1310720 | tf_op jit(solution)/shard_map/all_gather | solution.py:93
  67.7 1.7 copy-start.17
  69.4 1.9 copy-start.18
  71.3 5.5 %copy-start.1 = (f32[2,64,32,64]{3,1,2,0:T(8,128)}, f32[2,64,32,64]{3,1,2,0:T(8,128)S(1)}, u32[]{:S(2)}) copy-start(f32[2,64,32,64]{3,1,2,0:T(8,128)S(1)} %fusion.13) | copy-start | bytes 3145732
  71.3 1.9 copy-start.8
  71.3 1.9 copy-start.9
  73.1 3.6 copy-start.3
  85.2 0.8 copy-start.12
  87.4 14.9 %all-to-all-start.2 = ((f32[1,256,512]{1,0,2:T(1,128)}), f32[1,256,512]{1,0,2:T(1,128)S(1)}, u32[]{:S(2)}, u32[]{:S(2)}) async-start(f32[1,256,512]{1,0,2:T(1,128)} %copy.165), calls=%async_computation.3 | async-start | bytes 1048576 | tf_op jit(solution)/shard_map/all_to_all | solution.py:79
  92.1 5.4 %copy-start.2 = (f32[2,64,32,64]{3,1,2,0:T(8,128)S(1)}, f32[2,64,32,64]{3,1,2,0:T(8,128)}, u32[]{:S(2)}) copy-start(f32[2,64,32,64]{3,1,2,0:T(8,128)} %copy-done.1) | copy-start | bytes 3145732
  92.1 5.4 %copy-start.4 = (f32[2,64,32,64]{3,1,2,0:T(8,128)S(1)}, f32[2,64,32,64]{3,1,2,0:T(8,128)}, u32[]{:S(2)}) copy-start(f32[2,64,32,64]{3,1,2,0:T(8,128)} %copy-done.3) | copy-start | bytes 3145732
  102.3 2.4 copy-start.19
  103.4 3.1 copy-start.20
  111.9 2.0 copy-start.10
  112.0 2.2 copy-start.11
  160.3 46.7 %all-to-all-start.1 = ((f32[16,1,8192]{2,1,0:T(1,128)}), f32[16,1,8192]{2,1,0:T(1,128)}, u32[]{:S(2)}, u32[]{:S(2)}) async-start(f32[16,1,8192]{2,1,0:T(1,128)} %reshape.238), calls=%async_computation.1 | async-start | bytes 1048576 | tf_op jit(solution)/shard_map/all_to_all | solution.py:83
  166.5 4.0 copy-start.6
  166.5 4.0 copy-start.7
  207.1 19.7 %all-to-all-start.3 = ((f32[16,1,8192]{2,1,0:T(1,128)}), f32[16,1,8192]{2,1,0:T(1,128)}, u32[]{:S(2)}, u32[]{:S(2)}) async-start(f32[16,1,8192]{2,1,0:T(1,128)} %reshape.240), calls=%async_computation.4 | async-start | bytes 1048576 | tf_op jit(solution)/shard_map/all_to_all | solution.py:83
  212.8 39.5 %all-reduce.4.cloned.1.call-start = ((), (), s32[]{:S(2)}) async-start(), calls=%async_computation.7 | async-start | bytes 1048576 | tf_op jit(solution)/shard_map/psum | solution.py:130
  215.6 172.5 %all-reduce.6.cloned.1.call-start = ((), (), s32[]{:S(2)}) async-start(), calls=%async_computation.9 | async-start | bytes 14680064 | tf_op jit(solution)/shard_map/psum | solution.py:145
  234.4 2.7 copy-start.13
  234.4 2.7 copy-start.28
  237.1 1.9 copy-start.26
  238.9 2.4 copy-start.21
  238.9 2.4 copy-start.23
  239.0 3.4 copy-start.14
  245.2 173.7 %reduce-scatter.2.cloned.1.call-start = ((), (), s32[]{:S(2)}) async-start(), calls=%async_computation.6 | async-start | bytes 2621440 | tf_op jit(solution)/shard_map/reduce_scatter | solution.py:111
  252.2 3.9 slice-start
  255.9 1.1 copy-start.15
  267.9 79.7 %copy-start.22 = (bf16[1,256,512]{1,2,0:T(8,128)(2,1)S(1)}, bf16[1,256,512]{1,2,0:T(8,128)(2,1)}, u32[]{:S(2)}) copy-start(bf16[1,256,512]{1,2,0:T(8,128)(2,1)} %copy-done.21) | copy-start | bytes 786436
  267.9 79.7 %copy-start.24 = (bf16[1,256,512]{1,2,0:T(8,128)(2,1)S(1)}, bf16[1,256,512]{1,2,0:T(8,128)(2,1)}, u32[]{:S(2)}) copy-start(bf16[1,256,512]{1,2,0:T(8,128)(2,1)} %copy-done.23) | copy-start | bytes 786436
  267.9 82.4 %all-to-all-start.4 = ((f32[16,1,16384]{2,1,0:T(1,128)}), f32[16,1,16384]{2,1,0:T(1,128)}, u32[]{:S(2)}, u32[]{:S(2)}) async-start(f32[16,1,16384]{2,1,0:T(1,128)} %reshape.242), calls=%async_computation.5 | async-start | bytes 2097152 | tf_op jit(solution)/shard_map/all_to_all | solution.py:83
  364.3 1.3 copy-start.16
Sparse Core Ops, SparseCore 0:
  26.4 25.0 all-gather.2
  216.0 36.1 all-reduce.3
  256.4 131.7 all-reduce.5
  390.4 28.4 reduce-scatter.1

commit v2 on v1

--- a/solution.py
+++ b/solution.py
@@ -12,8 +12,8 @@
 
 
 def factor_split(length):
-    first = 1 << (int(math.log2(length)) // 2)
-    return first, length // first
+    second = 256
+    return length // second, second
 
 
 def unit_table(size):
@@ -34,37 +34,33 @@
 
 
 def real_spectrum(signal):
-    field_count, length, width = signal.shape
+    field_count, width, length = signal.shape
     first, second = factor_split(length)
-    grid = signal.reshape(field_count, first, second, width)
+    grid = signal.reshape(field_count, width, first, second)
     cos_a, sin_a = unit_table(first)
     cos_b, sin_b = unit_table(second)
     cos_t, sin_t = twiddle_table(first, second)
-    y_re = table_apply(cos_a, grid, "kn,fnmc->fkmc")
-    y_im = -table_apply(sin_a, grid, "kn,fnmc->fkmc")
-    cos_t = cos_t[None, :, :, None]
-    sin_t = sin_t[None, :, :, None]
+    y_re = table_apply(cos_a, grid, "kn,fcnm->fckm")
+    y_im = -table_apply(sin_a, grid, "kn,fcnm->fckm")
     z_re = y_re * cos_t + y_im * sin_t
     z_im = y_im * cos_t - y_re * sin_t
-    x_re = table_apply(cos_b, z_re, "jm,fkmc->fjkc") + table_apply(sin_b, z_im, "jm,fkmc->fjkc")
-    x_im = table_apply(cos_b, z_im, "jm,fkmc->fjkc") - table_apply(sin_b, z_re, "jm,fkmc->fjkc")
+    x_re = table_apply(cos_b, z_re, "jm,fckm->fckj") + table_apply(sin_b, z_im, "jm,fckm->fckj")
+    x_im = table_apply(cos_b, z_im, "jm,fckm->fckj") - table_apply(sin_b, z_re, "jm,fckm->fckj")
     return x_re, x_im
 
 
 def real_inverse(spec_re, spec_im):
-    field_count, second, first, width = spec_re.shape
+    field_count, width, first, second = spec_re.shape
     length = first * second
     cos_a, sin_a = unit_table(first)
     cos_b, sin_b = unit_table(second)
     cos_t, sin_t = twiddle_table(first, second)
-    a_re = table_apply(cos_b, spec_re, "mj,fjkc->fmkc") - table_apply(sin_b, spec_im, "mj,fjkc->fmkc")
-    a_im = table_apply(cos_b, spec_im, "mj,fjkc->fmkc") + table_apply(sin_b, spec_re, "mj,fjkc->fmkc")
-    cos_t = cos_t.T[None, :, :, None]
-    sin_t = sin_t.T[None, :, :, None]
+    a_re = table_apply(cos_b, spec_re, "mj,fckj->fckm") - table_apply(sin_b, spec_im, "mj,fckj->fckm")
+    a_im = table_apply(cos_b, spec_im, "mj,fckj->fckm") + table_apply(sin_b, spec_re, "mj,fckj->fckm")
     b_re = a_re * cos_t - a_im * sin_t
     b_im = a_re * sin_t + a_im * cos_t
-    out = table_apply(cos_a, b_re, "nk,fmkc->fnmc") - table_apply(sin_a, b_im, "nk,fmkc->fnmc")
-    return out.reshape(field_count, length, width) * (1.0 / length)
+    out = table_apply(cos_a, b_re, "nk,fckm->fcnm") - table_apply(sin_a, b_im, "nk,fckm->fcnm")
+    return out.reshape(field_count, width, length) * (1.0 / length)
 
 
 def lag_reverse(signal, axis):
@@ -76,11 +72,34 @@
 
 
 def to_channels(fields):
-    return lax.all_to_all(fields, "seq", split_axis=2, concat_axis=1, tiled=True)
+    return lax.all_to_all(
+        jnp.swapaxes(fields, 1, 2), "seq", split_axis=1, concat_axis=2, tiled=True
+    )
 
 
 def to_rows(fields):
-    return lax.all_to_all(fields, "seq", split_axis=1, concat_axis=2, tiled=True)
+    gathered = lax.all_to_all(fields, "seq", split_axis=2, concat_axis=1, tiled=True)
+    return jnp.swapaxes(gathered, 1, 2)
+
+
+def rep_sum(value):
+    count = lax.axis_size("rep")
+    total = value
+    for shift in range(1, count):
+        pairs = [(i, (i + shift) % count) for i in range(count)]
+        total = total + lax.ppermute(value, "rep", pairs)
+    return total
+
+
+def chan_reduce_scatter(terms):
+    count = lax.axis_size("chan")
+    rows, total_width = terms.shape
+    pieces = terms.reshape(rows, count, total_width // count).transpose(1, 0, 2)
+    received = lax.all_to_all(pieces, "chan", split_axis=0, concat_axis=0, tiled=True)
+    total = received[0]
+    for index in range(1, count):
+        total = total + received[index]
+    return total
 
 
 def on_device(inputs, w_in, w_out, filt_fwd, filt_bwd, skip_gain, cotangent):
@@ -99,7 +118,7 @@
     mixed = keys * values
     spread = to_channels(jnp.stack([mixed, filt_fwd, filt_bwd]))
     mixed_cs = spread[0]
-    joint_filter = spread[1] + lag_reverse(spread[2], 0)
+    joint_filter = spread[1] + lag_reverse(spread[2], 1)
     spec_re, spec_im = real_spectrum(jnp.stack([mixed_cs, joint_filter]))
     mix_re, mix_im = (spec_re[0], spec_im[0])
     gain_re, gain_im = (spec_re[1], spec_im[1])
@@ -108,18 +127,19 @@
     conv_out = long_conv + skip_gain * mixed
     gated = (queries * conv_out).astype(jnp.bfloat16)
     out_terms = jnp.dot(gated, w_out, preferred_element_type=jnp.float32)
-    layer_out = lax.psum_scatter(out_terms, "chan", scatter_dimension=1, tiled=True).astype(
-        jnp.bfloat16
-    )
+    layer_out = chan_reduce_scatter(out_terms).astype(jnp.bfloat16)
     grad_gated = lax.dot_general(
         piece, w_out, (((1,), (1,)), ((), ())), preferred_element_type=jnp.float32
     )
     grad_wout = lax.dot_general(
         gated, piece, (((0,), (0,)), ((), ())), preferred_element_type=jnp.float32
     )
-    grad_wout = lax.psum(grad_wout, ("seq", "rep"))
     grad_queries = grad_gated * conv_out
     grad_conv = grad_gated * queries
+    grad_skip = jnp.sum(grad_conv * mixed, axis=0)
+    out_width = grad_wout.shape[1]
+    skip_row = jnp.pad(grad_skip, (0, out_width - chan_width))[None]
+    early_sums = lax.psum(jnp.concatenate([grad_wout, skip_row], axis=0), ("seq", "rep"))
     grad_cs = to_channels(grad_conv[None])
     grad_re, grad_im = real_spectrum(grad_cs)
     grad_re, grad_im = (grad_re[0], grad_im[0])
@@ -127,8 +147,8 @@
     cross_re, cross_im = complex_product(grad_re, grad_im, mix_re, -mix_im)
     results = real_inverse(jnp.stack([back_re, cross_re]), jnp.stack([back_im, cross_im]))
     back = to_rows(results[0][None])[0]
-    grad_hfwd = lax.psum(results[1], "rep")
-    grad_hbwd = lag_reverse(grad_hfwd, 0)
+    grad_hfwd = rep_sum(results[1])
+    grad_hbwd = lag_reverse(grad_hfwd, 1)
     filt_grads = to_rows(jnp.stack([grad_hfwd, grad_hbwd]))
     grad_mixed = back + skip_gain * grad_conv
     grad_pre = jnp.stack([grad_mixed * values, grad_mixed * keys, grad_queries]).astype(
@@ -137,12 +157,14 @@
     pre_blocks = grad_pre.reshape(3, row_count, block_count, BLOCK)
     d_input = jnp.einsum("smnj,nisj->mni", pre_blocks, w_blocks, preferred_element_type=jnp.float32)
     d_input = d_input.reshape(row_count, chan_width).astype(jnp.bfloat16)
+    pre_late, early_sums = lax.optimization_barrier((pre_blocks, early_sums))
     grad_win = jnp.einsum(
-        "mni,smnj->nisj", input_blocks, pre_blocks, preferred_element_type=jnp.float32
+        "mni,smnj->nisj", input_blocks, pre_late, preferred_element_type=jnp.float32
     )
     grad_win = grad_win.reshape(chan_width, 3 * BLOCK)
-    grad_skip = jnp.sum(grad_conv * mixed, axis=0)
-    grad_win, grad_skip = lax.psum((grad_win, grad_skip), ("seq", "rep"))
+    grad_win = lax.psum(grad_win, ("seq", "rep"))
+    grad_wout = early_sums[:chan_width]
+    grad_skip = early_sums[chan_width, :chan_width]
     scale = 1.0 / math.sqrt(lax.axis_size("rep") * lax.axis_size("seq") * row_count)
     return (
         layer_out[None],

time: 434 us -> 462 us (1.065)
  waiting for transfers between devices: 70.9 us -> 193 us
  blocking collectives: 73.1 us -> 14.2 us
  matrix products: 77.9 us -> 37.2 us
    psum x2, waiting for transfers between devices: 25.9 us -> 155 us  [the longest x1 83.1 us: on_device(): grad_win = lax.psum(grad_win, ('seq', 'rep'))]
    psum x1 -> x0, blocking collectives: 73.1 us -> none  [on_device(): grad_win, grad_skip = lax.psum((grad_win, grad_skip), ('seq', 'rep'))]
    dot_general x24, matrix products: 62.9 us -> 20.7 us  [table_apply(): return jnp.einsum(form, table, fields, precision=HIGHEST_PRECISION)]
    reduce_scatter x1 -> x0, waiting for transfers between devices: 18.3 us -> none  [on_device(): lax.psum_scatter(out_terms, 'chan', scatter_dimension=1, tiled=True)]
    all_to_all x0 -> x1, blocking collectives: none -> 14.2 us  [to_rows(): lax.all_to_all(fields, 'seq', split_axis=2, concat_axis=1, tiled=True)]
    unnamed x75 -> x79, local copies, waits for them, and re-layouts: 45.9 us -> 59.1 us
    ppermute x0 -> x1, waiting for transfers between devices: none -> 8.95 us  [rep_sum(): total = total + lax.ppermute(value, 'rep', pairs)]
    another operation x4 -> x0, local copies, waits for them, and re-layouts: 7.42 us -> none  [the longest x2 3.78 us: on_device(): spec_re, spec_im = real_spectrum(jnp.stack([mixed_cs, joint_filter]))]
  transfers between devices with their start and end apart: 9 -> 9, of which waited for: 4 -> 6; matrix products, arithmetic and copies ran while one was open for 38% -> 32% of each run, Pallas kernels for 0% -> 0%
where the time goes in v2:
time: 462 us; the launch traced here: 456 us
  waiting for transfers between devices  193 us (42%)
  local copies, waits for them, and re-layouts  96.6 us (21%)
  other arithmetic  71.4 us (15%)
  matrix products  37.2 us (8%)
  starting transfers between devices  28.5 us (6%)
  between operations  14.7 us (3%)
  blocking collectives  14.2 us (3%)
    psum x1, waiting for transfers between devices, on_device(): grad_win = lax.psum(grad_win, ('seq', 'rep'))  83.1 us
    psum x1, waiting for transfers between devices, on_device(): lax.psum(jnp.concatenate([grad_wout, skip_row], axis=0), ('seq', 'rep'))  71.5 us
    unnamed x79, local copies, waits for them, and re-layouts  59.1 us
    unnamed x2, other arithmetic  41.3 us
    all_to_all x2, waiting for transfers between devices, to_channels(): lax.all_to_all(jnp.swapaxes(fields, 1, 2), 'seq', split_axis=1, concat_ax...  27.6 us
    dot_general x24, matrix products, table_apply(): return jnp.einsum(form, table, fields, precision=HIGHEST_PRECISION)  20.7 us
    all_to_all x1, blocking collectives, to_rows(): lax.all_to_all(fields, 'seq', split_axis=2, concat_axis=1, tiled=True)  14.2 us
    all_to_all x7, local copies, waits for them, and re-layouts, to_rows(): lax.all_to_all(fields, 'seq', split_axis=2, concat_axis=1, tiled=True)  13.4 us
  transfers between devices with their start and end apart: 9, of which 6 were waited for; matrix products, arithmetic and copies ran while one was open for 32% of the time, Pallas kernels for 0%

profile of v2, /device:TPU:6, one launch (start us, length us, event | category | flops | bytes accessed | tf_op | source)
XLA Modules:
  0.0 455.5 jit_solution(10700167182240753181)
XLA Ops:
  7.2 1.8 copy.124
  10.9 1.8 copy.129
  12.6 6.8 %all-to-all-start = ((f32[3,512,256]{2,0,1:T(4,128)}), f32[3,512,256]{2,0,1:T(4,128)}, u32[]{:S(2)}, u32[]{:S(2)}) async-start(f32[3,512,256]{2,0,1:T(4,128)} %copy.129), calls=%async_computation | async-start | bytes 4194304 | tf_op jit(solution)/shard_map/all_to_all | solution.py:75
  20.2 26.0 %all-to-all-done = f32[3,512,256]{2,0,1:T(4,128)} async-done(((f32[3,512,256]{2,0,1:T(4,128)}), f32[3,512,256]{2,0,1:T(4,128)}, u32[]{:S(2)}, u32[]{:S(2)}) %all-to-all-start) | async-done | bytes 1572896 | tf_op jit(solution)/shard_map/all_to_all | solution.py:75
  46.1 2.5 copy.182
  50.9 15.8 %reverse.4 = f32[32,4096]{1,0:T(8,128)} reverse(f32[32,4096]{1,0:T(8,128)} %bitcast.313), dimensions={1} | reverse | bytes 1048576
  66.7 2.0 slice_bitcast_fusion
  81.7 2.0 copy.161
  84.2 20.9 %reduce = f32[4096,32]{1,0:T(8,128)} reduce(f32[4096,1,32]{2,1,0:T(1,128)} %bitcast.291, f32[]{:T(128)} %broadcast.52), dimensions={1}, to_apply=%bitcast.234.reduce_sub_computation | reduce | bytes 1048580
  105.1 2.5 reshape.272
  107.5 14.2 %all_to_all.89 = f32[16,1,8192]{2,1,0:T(1,128)} all-to-all(f32[16,1,8192]{2,1,0:T(1,128)S(1)} %reshape.272), channel_id=1, replica_groups=mesh['seq'=16,'chan'=4,'rep'=2] {'seq'}, dimensions={0} | all-to-all | bytes 1048576 | tf_op jit(solution)/shard_map/all_to_all | solution.py:81
  121.7 3.0 reduce.1
  124.6 4.8 %reshape.273 = f32[4096,1,32]{2,1,0:T(1,128)} reshape(f32[16,8192]{1,0:T(8,128)S(1)} %reduce.1) | data formatting | bytes 1048576
  129.4 2.3 copy.162
  134.1 3.6 multiply_reduce_fusion
  137.7 1.9 copy.139
  139.6 5.2 %all-to-all-start.3 = ((f32[1,512,256]{2,0,1:T(1,128)}), f32[1,512,256]{2,0,1:T(1,128)}, u32[]{:S(2)}, u32[]{:S(2)}) async-start(f32[1,512,256]{2,0,1:T(1,128)} %copy.139), calls=%async_computation.3 | async-start | bytes 1048576 | tf_op jit(solution)/shard_map/all_to_all | solution.py:75
  144.9 4.1 copy.163
  148.9 4.1 fusion.10
  153.1 1.6 all-to-all-done.3
  167.7 2.2 copy.164
  169.9 20.4 %reduce.2 = f32[4096,32]{1,0:T(8,128)} reduce(f32[4096,1,32]{2,1,0:T(1,128)} %bitcast.292, f32[]{:T(128)} %broadcast.52), dimensions={1}, to_apply=%bitcast.236.reduce_sub_computation | reduce | bytes 1048580
  190.3 3.1 reshape.274
  193.4 4.6 %all-to-all-start.4 = ((f32[16,1,8192]{2,1,0:T(1,128)}), f32[16,1,8192]{2,1,0:T(1,128)S(1)}, u32[]{:S(2)}, u32[]{:S(2)}) async-start(f32[16,1,8192]{2,1,0:T(1,128)} %reshape.274), calls=%async_computation.4 | async-start | bytes 1048576 | tf_op jit(solution)/shard_map/all_to_all | solution.py:81
  198.1 4.8 %pad_maximum_fusion = f32[513,2048]{1,0:T(8,128)} fusion(f32[1,2048]{1,0:T(1,128)S(1)} %bitcast.328, f32[512,2048]{1,0:T(8,128)} %fusion.10), kind=kLoop, calls=%fused_computation | loop fusion | flops 1050624 | bytes 8404992 | tf_op jit(solution)/shard_map/concatenate | solution.py:142
  202.9 3.7 convolution_bitcast_fusion.1
  207.8 4.5 all-to-all-start.2
  212.6 1.9 collective-permute-start
  214.5 1.9 reduce.3
  216.4 4.8 %reshape.275 = f32[4096,1,32]{2,1,0:T(1,128)} reshape(f32[16,8192]{1,0:T(8,128)S(1)} %reduce.3) | data formatting | bytes 1048576
  221.2 2.3 copy.165
  224.9 8.9 %collective-permute-done = f32[32,4096]{1,0:T(8,128)} collective-permute-done((f32[32,4096]{1,0:T(8,128)S(1)}, f32[32,4096]{1,0:T(8,128)}, u32[]{:S(2)}, u32[]{:S(2)}) %collective-permute-start) | collective-permute-done | bytes 524320 | tf_op jit(solution)/shard_map/ppermute | solution.py:90
  235.1 2.3 reverse.5
  238.0 4.4 copy.147
  242.4 6.5 %reshape.276 = f32[16,1,16384]{2,1,0:T(1,128)} reshape(f32[4096,2,32]{2,1,0:T(2,128)} %bitcast.287) | data formatting | bytes 2097152
  248.9 5.2 %all-to-all-start.5 = ((f32[16,1,16384]{2,1,0:T(1,128)}), f32[16,1,16384]{2,1,0:T(1,128)S(1)}, u32[]{:S(2)}, u32[]{:S(2)}) async-start(f32[16,1,16384]{2,1,0:T(1,128)} %reshape.276), calls=%async_computation.5 | async-start | bytes 2097152 | tf_op jit(solution)/shard_map/all_to_all | solution.py:81
  256.5 71.5 %all-reduce.4.cloned.1.call-done = f32[513,2048]{1,0:T(8,128)} async-done(((f32[513,2048]{1,0:T(8,128)}), f32[513,2048]{1,0:T(8,128)}) %all-reduce.4.cloned.1.call-update) | async-done | bytes 4202512 | tf_op jit(solution)/shard_map/psum | solution.py:142
  328.3 2.2 convolution_bitcast_fusion
  330.6 1.4 copy-done.4
  332.1 2.2 fusion.9
  334.3 2.4 fusion.30
  336.7 3.2 reduce.4
  339.8 4.9 %reshape.277 = f32[4096,2,32]{2,1,0:T(2,128)} reshape(f32[16,16384]{1,0:T(8,128)S(1)} %reduce.4) | data formatting | bytes 2097152
  344.7 5.2 %copy.167 = f32[2,32,16,256]{3,1,2,0:T(8,128)S(1)} copy(f32[2,32,16,256]{1,0,3,2:T(2,128)} %bitcast.288) | data formatting | bytes 2097152 | tf_op jit(solution)/shard_map/all_to_all | solution.py:81
  353.3 5.0 %slice_multiply_fusion = f32[512,2048]{1,0:T(8,128)} fusion(f32[513,2048]{1,0:T(8,128)} %all-reduce.4.cloned.1.call-done), kind=kLoop, calls=%fused_computation.1 | loop fusion | flops 1048576 | bytes 8388608 | tf_op jit(solution)/shard_map/mul | solution.py:173
  358.3 83.1 %all-reduce.6.cloned.1.call-done = f32[512,1536]{0,1:T(8,128)} async-done(((f32[512,1536]{0,1:T(8,128)}), f32[512,1536]{0,1:T(8,128)}) %all-reduce.6.cloned.1.call-update) | async-done | bytes 3145744 | tf_op jit(solution)/shard_map/psum | solution.py:165
  441.4 3.9 broadcast_multiply_fusion
  445.3 3.5 copy.150
  (128 shorter events, 44.1 us)
Async XLA Ops:
  7.2 1.8 copy-start
  8.9 1.1 copy-start.3
  9.0 1.4 copy-start.23
  9.0 1.8 copy-start.24
  12.6 33.5 %all-to-all-start = ((f32[3,512,256]{2,0,1:T(4,128)}), f32[3,512,256]{2,0,1:T(4,128)}, u32[]{:S(2)}, u32[]{:S(2)}) async-start(f32[3,512,256]{2,0,1:T(4,128)} %copy.129), calls=%async_computation | async-start | bytes 4194304 | tf_op jit(solution)/shard_map/all_to_all | solution.py:75
  19.4 114.7 %all-gather.3.cloned.1.call-start = ((), (), s32[]{:S(2)}) async-start(), calls=%async_computation.8 | async-start | bytes 1310720 | tf_op jit(solution)/shard_map/all_gather | solution.py:112
  68.7 1.7 copy-start.26
  68.8 1.6 copy-start.6
  70.3 1.2 copy-start.27
  70.4 2.1 copy-start.11
  70.4 2.1 copy-start.15
  70.4 2.1 copy-start.16
  73.6 1.0 copy-start.9
  76.7 1.8 copy-start.1
  76.7 1.1 copy-start.7
  77.0 2.1 copy-start.13
  79.1 1.3 copy-start.28
  79.7 1.3 copy-start.29
  129.4 4.7 %copy-start.25 = (f32[512]{0:T(512)S(1)}, f32[512]{0:T(512)}, u32[]{:S(2)}) copy-start(f32[512]{0:T(512)} %param.36) | copy-start | bytes 6148
  139.6 15.1 %all-to-all-start.3 = ((f32[1,512,256]{2,0,1:T(1,128)}), f32[1,512,256]{2,0,1:T(1,128)}, u32[]{:S(2)}, u32[]{:S(2)}) async-start(f32[1,512,256]{2,0,1:T(1,128)} %copy.139), calls=%async_computation.3 | async-start | bytes 1048576 | tf_op jit(solution)/shard_map/all_to_all | solution.py:75
  154.7 2.9 copy-start.8
  157.6 1.3 copy-start.14
  158.2 1.3 copy-start.2
  159.5 1.0 copy-start.12
  160.5 2.1 copy-start.10
  193.4 14.4 %all-to-all-start.4 = ((f32[16,1,8192]{2,1,0:T(1,128)}), f32[16,1,8192]{2,1,0:T(1,128)S(1)}, u32[]{:S(2)}, u32[]{:S(2)}) async-start(f32[16,1,8192]{2,1,0:T(1,128)} %reshape.274), calls=%async_computation.4 | async-start | bytes 1048576 | tf_op jit(solution)/shard_map/all_to_all | solution.py:81
  198.1 130.0 %all-reduce.4.cloned.1.call-start = ((), (), s32[]{:S(2)}) async-start(), calls=%async_computation.6 | async-start | bytes 8519680 | tf_op jit(solution)/shard_map/psum | solution.py:142
  206.6 5.7 %copy-start.17 = (f32[1,32,16,256]{3,2,1,0:T(8,128)S(1)}, f32[1,32,16,256]{3,2,1,0:T(8,128)}, u32[]{:S(2)}) copy-start(f32[1,32,16,256]{3,2,1,0:T(8,128)} %get-tuple-element.61) | copy-start | bytes 1572868
  207.8 41.1 %all-to-all-start.2 = ((f32[4,256,512]{2,1,0:T(8,128)}), f32[4,256,512]{2,1,0:T(8,128)}, u32[]{:S(2)}, u32[]{:S(2)}) async-start(f32[4,256,512]{2,1,0:T(8,128)} %convolution_bitcast_fusion.1), calls=%async_computation.2 | async-start | bytes 4194304 | tf_op jit(solution)/shard_map/all_to_all | solution.py:98
  212.6 21.2 %collective-permute-start = (f32[32,4096]{1,0:T(8,128)S(1)}, f32[32,4096]{1,0:T(8,128)}, u32[]{:S(2)}, u32[]{:S(2)}) collective-permute-start(f32[32,4096]{1,0:T(8,128)S(1)} %bitcast.308), channel_id=1, source_target_pairs={{0,1},{1,0},{2,3},{3,2},{4,5},{5,4},{6,7},{7,6},{8,9},{9,8},{10,11... | collective-permute-start | bytes 1572872 | tf_op jit(solution)/shard_map/ppermute | solution.py:90
  248.9 5.4 %copy-start.5 = (f32[256,512]{1,0:T(8,128)S(1)}, f32[256,512]{1,0:T(8,128)}, u32[]{:S(2)}) copy-start(f32[256,512]{1,0:T(8,128)} %get-tuple-element.47) | copy-start | bytes 1572868
  248.9 87.8 %all-to-all-start.5 = ((f32[16,1,16384]{2,1,0:T(1,128)}), f32[16,1,16384]{2,1,0:T(1,128)S(1)}, u32[]{:S(2)}, u32[]{:S(2)}) async-start(f32[16,1,16384]{2,1,0:T(1,128)} %reshape.276), calls=%async_computation.5 | async-start | bytes 2097152 | tf_op jit(solution)/shard_map/all_to_all | solution.py:81
  254.1 187.3 %all-reduce.6.cloned.1.call-start = ((), (), s32[]{:S(2)}) async-start(), calls=%async_computation.7 | async-start | bytes 6291456 | tf_op jit(solution)/shard_map/psum | solution.py:165
  254.3 2.1 copy-start.18
  255.6 0.7 copy-start.20
  255.6 0.8 copy-start.22
  330.6 1.4 copy-start.4
  330.6 1.4 copy-start.19
  330.6 1.5 copy-start.21
Sparse Core Ops, SparseCore 0:
  21.9 25.0 all-gather.2
  203.0 124.9 all-reduce.3
  332.0 109.3 all-reduce.5
